TPU v7x, 256 devices: a whole 4x4x8 slice. The times are simulated.
256 devices in a mesh: ctx: 32 (over x, z_lo, core), tp: 8 (over z_hi, y).
Axes of the slice: x: 4, y: 4, z: 8 (z_hi: 2, z_lo: 4; z = z_hi * 4 + z_lo), core: 2. Of those that a mesh axis runs over, the one named last changes fastest.
Arguments:
- queries: bfloat16 [8192, 8192], P('ctx', 'tp'), may hold values from -8 to 8
- key_rows: bfloat16 [8192, 1024], P('ctx', 'tp'), may hold values from -8 to 8
- value_head_rows: bfloat16 [8192, 1024], P('ctx', 'tp'), may hold values from -6 to 6
- ssm_input: bfloat16 [8192, 8192], P('ctx', 'tp'), may hold values from -6 to 6
- gate_input: bfloat16 [8192, 8192], P('ctx', 'tp'), may hold values from -6 to 6
- b_matrix: bfloat16 [8192, 1024], P('ctx', 'tp'), may hold values from -6 to 6
- c_matrix: bfloat16 [8192, 1024], P('ctx', 'tp'), may hold values from -0.5 to 0.5
- step_size: float32 [128, 8192], P('tp', 'ctx'), may hold values from 0.02 to 0.2
- log_decay: float32 [128, 8192], P('tp', 'ctx'), may hold values from -1.5 to 0
- skip_gain: float32 [128], P('tp'), may hold values from 0.5 to 1.5
- norm_gain: bfloat16 [8192], P('tp'), may hold values from 0.099609375 to 1.8984375
Outputs:
- attention_out: bfloat16 [8192, 8192], P('ctx', 'tp')
- mixer_out: bfloat16 [8192, 8192], P('ctx', 'tp')
All inputs are finite; a program needn't handle non-finite values.
Results may differ from a plain program's by a relative error of at most 0.022.
Values may be sent and summed in bfloat16 or wider, within the bound.
No kernel may reach another device: no remote copies, remote signals or barrier semaphores. Data moves between devices by JAX's collectives and lax.ppermute only.
A program may use at most 128 MiB of HBM per device.

v0:
```python
import math
import jax
import jax.numpy as jnp
from jax import lax
from jax.sharding import PartitionSpec as P

HEAD_WIDTH = 128
STATE_HEADS = 128
P_SIZE = 64
N = 128
causal_score = -1e30


def passed_along(block, axis, distance):
    devices = range(lax.axis_size(axis))
    route = [(i - distance, i) for i in devices if i - distance in devices]
    return lax.ppermute(block, axis, route)


def attend_rows(running_in, key_block, value_block, key_start, query_head_rows, query_pos):
    row_count = key_block.shape[0]
    sub_width = math.gcd(row_count, 512)
    kv_heads = query_head_rows.shape[1]
    score_factor = query_head_rows.shape[3] ** (-0.5)

    def sub_step(sub_id, running):
        run_max, run_sum, summed_so_far = running
        offset = sub_id * sub_width
        key_portion = key_block.reshape(sub_width, kv_heads, -1)
        value_portion = value_block.reshape(sub_width, kv_heads, -1)
        key_pos = key_start + offset + jnp.arange(sub_width, dtype=jnp.int32)
        is_valid = key_pos[None, :] <= query_pos[:, None]
        score_matrix = (
            jnp.einsum(
                "faqo,bao->aqfb", query_head_rows, key_portion, preferred_element_type=jnp.float32
            )
            * score_factor
        )
        score_matrix = jnp.where(is_valid, score_matrix, causal_score)
        new_max = jnp.maximum(run_max, jnp.max(score_matrix, axis=-1))
        weights = jnp.where(is_valid, jnp.exp(score_matrix - new_max[..., None]), 0.0)
        correction_factor = jnp.exp(run_max - new_max)
        run_sum = run_sum * correction_factor + jnp.sum(weights, axis=-1)
        summed_so_far = summed_so_far * correction_factor[..., None] + jnp.einsum(
            "wlhc,cwm->wlhm",
            weights.astype(jnp.bfloat16),
            value_portion,
            preferred_element_type=jnp.float32,
        )
        return (new_max, run_sum, summed_so_far)

    return lax.fori_loop(0, row_count // sub_width, sub_step, running_in)


def local(
    queries,
    key_rows,
    value_head_rows,
    ssm_input,
    gate_input,
    b_matrix,
    c_matrix,
    step_size,
    log_decay,
    skip_gain,
    norm_gain,
):
    tok_rows = queries.shape[0]
    kv_heads = key_rows.shape[1] // HEAD_WIDTH
    query_per_key_heads = queries.shape[1] // HEAD_WIDTH // kv_heads
    query_head_rows = queries.reshape(tok_rows, kv_heads, query_per_key_heads, HEAD_WIDTH)
    ctx_count = lax.axis_size("ctx")
    position = lax.axis_index("ctx")
    query_pos = position * tok_rows + jnp.arange(tok_rows, dtype=jnp.int32)
    starting_state = (
        jnp.full((kv_heads, query_per_key_heads, tok_rows), causal_score, jnp.float32),
        jnp.zeros((kv_heads, query_per_key_heads, tok_rows), jnp.float32),
        jnp.zeros((kv_heads, query_per_key_heads, tok_rows, HEAD_WIDTH), jnp.float32),
    )
    first_pass = attend_rows(
        starting_state, key_rows, value_head_rows, position * tok_rows, query_head_rows, query_pos
    )

    def cycle_step(step_id, state):
        stacked, running = state
        stacked = passed_along(stacked, "ctx", 1)
        sender_index = position - step_id
        key_start = jnp.where(sender_index >= 0, sender_index * tok_rows, ctx_count * tok_rows)
        return (
            stacked,
            attend_rows(running, stacked[0], stacked[1], key_start, query_head_rows, query_pos),
        )

    _, (run_max, run_sum, summed_so_far) = lax.fori_loop(
        1, ctx_count, cycle_step, (jnp.stack((key_rows, value_head_rows)), first_pass)
    )
    attention_out = (
        (summed_so_far / run_sum[..., None])
        .transpose(2, 0, 1, 3)
        .reshape(tok_rows, -1)
        .astype(jnp.bfloat16)
    )
    heads_local = step_size.shape[0]
    groups_local = b_matrix.shape[1] // N
    heads_group = heads_local // groups_local
    mixer_in = ssm_input.reshape(tok_rows, groups_local, heads_group, P_SIZE)
    in_maps = b_matrix.reshape(tok_rows, groups_local, N)
    out_maps = c_matrix.reshape(tok_rows, groups_local, N)
    steps_here = step_size.reshape(groups_local, heads_group, tok_rows)
    cumul = jnp.cumsum(log_decay.reshape(groups_local, heads_group, tok_rows), axis=-1)
    causal = jnp.tril(jnp.ones((tok_rows, tok_rows), dtype=bool))
    gram = jnp.einsum("tgn,sgn->gts", out_maps, in_maps, preferred_element_type=jnp.float32)
    spread = jnp.where(causal, cumul[..., :, None] - cumul[..., None, :], 0.0)
    mixing = jnp.where(
        causal, gram[:, None] * jnp.exp(spread) * steps_here[..., None, :], 0.0
    ).astype(jnp.bfloat16)
    inner = jnp.einsum("ghts,sghp->tghp", mixing, mixer_in, preferred_element_type=jnp.float32)
    weight_end = jnp.exp(cumul[..., -1:] - cumul) * steps_here
    weighted = (mixer_in * weight_end.transpose(2, 0, 1)[..., None]).astype(jnp.bfloat16)
    local_state = jnp.einsum(
        "sghp,sgn->ghpn", weighted, in_maps, preferred_element_type=jnp.float32
    )
    block_decay = jnp.exp(cumul[..., -1])

    def relay_step(step_id, pair):
        received, outgoing = pair
        received = passed_along(outgoing.astype(jnp.bfloat16), "ctx", 1).astype(outgoing.dtype)
        return (received, block_decay[..., None, None] * received + local_state)

    incoming, _ = lax.fori_loop(
        1, ctx_count, relay_step, (jnp.zeros_like(local_state), local_state)
    )
    carried_out = jnp.einsum(
        "ghpn,tgn->tghp", incoming, out_maps.astype(jnp.float32), precision=lax.Precision.HIGHEST
    )
    carried_out = carried_out * jnp.exp(cumul).transpose(2, 0, 1)[..., None]
    direct = skip_gain.reshape(groups_local, heads_group)[None, :, :, None] * mixer_in.astype(
        jnp.float32
    )
    outputs = (inner + carried_out + direct).reshape(tok_rows, -1)
    gated = outputs * jax.nn.silu(gate_input.astype(jnp.float32))
    square_total = lax.psum(jnp.sum(gated * gated, axis=-1), "tp")
    scaling = lax.rsqrt(square_total / (STATE_HEADS * P_SIZE) + 1e-05)
    mixer_out = (gated * scaling[:, None] * norm_gain.astype(jnp.float32)).astype(jnp.bfloat16)
    return (attention_out, mixer_out)


def solution(mesh):
    placed = (
        P("ctx", "tp"),
        P("ctx", "tp"),
        P("ctx", "tp"),
        P("ctx", "tp"),
        P("ctx", "tp"),
        P("ctx", "tp"),
        P("ctx", "tp"),
        P("tp", "ctx"),
        P("tp", "ctx"),
        P("tp"),
        P("tp"),
    )
    return jax.shard_map(
        local,
        mesh=mesh,
        in_specs=placed,
        out_specs=(P("ctx", "tp"), P("ctx", "tp")),
        check_vma=False,
    )
```

profile of v0, /device:TPU:2, one launch (start us, length us, event | category | flops | bytes accessed | tf_op | source)
XLA Modules:
  0.0 740.2 jit_solution(10609625799831482986)
XLA Ops:
  5.4 343.8 %while.55 = (s32[]{:T(128)}, bf16[2,256,128]{2,1,0:T(8,128)(2,1)S(1)}, f32[1,8,256]{2,1,0:T(8,128)S(1)}, f32[1,8,256]{2,1,0:T(8,128)S(1)}, f32[1,8,256,128]{3,2,...) while((s32[]{:T(128)}, ...), condition=%wide.region_5.6_spmd.clone, body=%wide.region_2.5_spmd.clone.sunk | while | flops 275847680 | bytes 10227923 | solution.py:94
  353.0 347.9 %while.54 = (s32[]{:T(128)}, f32[1,16,64,128]{3,2,1,0:T(8,128)}, bf16[1,16,64,128]{3,2,1,0:T(8,128)(2,1)S(1)}, f32[1,16]{1,0:T(1,128)S(1)}, f32[1,16,64,128]{3,2,1,0:T(8,128)S(1)}, /*index=5*/s32[]{:T(128)}) while((s32[]{:T(128)}, f32[1,16,64,128]{3,2,1,0:T(8,128)}, bf16[1,16,64,128]{3,2,1,0:T(8,128)(2,1)S(1)}, f32[1,16]{1,0:T(1,128)S(1)}, ...), condition=%wide.region_9.10_spmd, body=%wide.region_8.9_spmd.sunk | while | flops 524290 | bytes 2621613 | solution.py:130
  366.1 8.5 %collective-permute-done = bf16[1,16,64,128]{3,2,1,0:T(8,128)(2,1)S(1)} collective-permute-done((bf16[1,16,64,128]{3,2,1,0:T(8,128)(2,1)S(1)}, bf16[1,16,64,128]{3,2,1,0:T(8,128)(2,1)S(1)}, u32[]{:S(2)}, u32[]{:S(2)}) %collective-permute-start) | collective-permute-done | bytes 262176 | tf_op jit(solution)/shard_map/while/body/eval_jaxpr/ppermute | solution.py:17
  377.4 8.5 %collective-permute-done = bf16[1,16,64,128]{3,2,1,0:T(8,128)(2,1)S(1)} collective-permute-done((bf16[1,16,64,128]{3,2,1,0:T(8,128)(2,1)S(1)}, bf16[1,16,64,128]{3,2,1,0:T(8,128)(2,1)S(1)}, u32[]{:S(2)}, u32[]{:S(2)}) %collective-permute-start) | collective-permute-done | bytes 262176 | tf_op jit(solution)/shard_map/while/body/eval_jaxpr/ppermute | solution.py:17
  399.8 8.5 %collective-permute-done = bf16[1,16,64,128]{3,2,1,0:T(8,128)(2,1)S(1)} collective-permute-done((bf16[1,16,64,128]{3,2,1,0:T(8,128)(2,1)S(1)}, bf16[1,16,64,128]{3,2,1,0:T(8,128)(2,1)S(1)}, u32[]{:S(2)}, u32[]{:S(2)}) %collective-permute-start) | collective-permute-done | bytes 262176 | tf_op jit(solution)/shard_map/while/body/eval_jaxpr/ppermute | solution.py:17
  411.0 8.5 %collective-permute-done = bf16[1,16,64,128]{3,2,1,0:T(8,128)(2,1)S(1)} collective-permute-done((bf16[1,16,64,128]{3,2,1,0:T(8,128)(2,1)S(1)}, bf16[1,16,64,128]{3,2,1,0:T(8,128)(2,1)S(1)}, u32[]{:S(2)}, u32[]{:S(2)}) %collective-permute-start) | collective-permute-done | bytes 262176 | tf_op jit(solution)/shard_map/while/body/eval_jaxpr/ppermute | solution.py:17
  433.4 8.5 %collective-permute-done = bf16[1,16,64,128]{3,2,1,0:T(8,128)(2,1)S(1)} collective-permute-done((bf16[1,16,64,128]{3,2,1,0:T(8,128)(2,1)S(1)}, bf16[1,16,64,128]{3,2,1,0:T(8,128)(2,1)S(1)}, u32[]{:S(2)}, u32[]{:S(2)}) %collective-permute-start) | collective-permute-done | bytes 262176 | tf_op jit(solution)/shard_map/while/body/eval_jaxpr/ppermute | solution.py:17
  444.7 8.5 %collective-permute-done = bf16[1,16,64,128]{3,2,1,0:T(8,128)(2,1)S(1)} collective-permute-done((bf16[1,16,64,128]{3,2,1,0:T(8,128)(2,1)S(1)}, bf16[1,16,64,128]{3,2,1,0:T(8,128)(2,1)S(1)}, u32[]{:S(2)}, u32[]{:S(2)}) %collective-permute-start) | collective-permute-done | bytes 262176 | tf_op jit(solution)/shard_map/while/body/eval_jaxpr/ppermute | solution.py:17
  455.9 8.5 %collective-permute-done = bf16[1,16,64,128]{3,2,1,0:T(8,128)(2,1)S(1)} collective-permute-done((bf16[1,16,64,128]{3,2,1,0:T(8,128)(2,1)S(1)}, bf16[1,16,64,128]{3,2,1,0:T(8,128)(2,1)S(1)}, u32[]{:S(2)}, u32[]{:S(2)}) %collective-permute-start) | collective-permute-done | bytes 262176 | tf_op jit(solution)/shard_map/while/body/eval_jaxpr/ppermute | solution.py:17
  478.3 8.5 %collective-permute-done = bf16[1,16,64,128]{3,2,1,0:T(8,128)(2,1)S(1)} collective-permute-done((bf16[1,16,64,128]{3,2,1,0:T(8,128)(2,1)S(1)}, bf16[1,16,64,128]{3,2,1,0:T(8,128)(2,1)S(1)}, u32[]{:S(2)}, u32[]{:S(2)}) %collective-permute-start) | collective-permute-done | bytes 262176 | tf_op jit(solution)/shard_map/while/body/eval_jaxpr/ppermute | solution.py:17
  489.5 8.5 %collective-permute-done = bf16[1,16,64,128]{3,2,1,0:T(8,128)(2,1)S(1)} collective-permute-done((bf16[1,16,64,128]{3,2,1,0:T(8,128)(2,1)S(1)}, bf16[1,16,64,128]{3,2,1,0:T(8,128)(2,1)S(1)}, u32[]{:S(2)}, u32[]{:S(2)}) %collective-permute-start) | collective-permute-done | bytes 262176 | tf_op jit(solution)/shard_map/while/body/eval_jaxpr/ppermute | solution.py:17
  512.0 8.5 %collective-permute-done = bf16[1,16,64,128]{3,2,1,0:T(8,128)(2,1)S(1)} collective-permute-done((bf16[1,16,64,128]{3,2,1,0:T(8,128)(2,1)S(1)}, bf16[1,16,64,128]{3,2,1,0:T(8,128)(2,1)S(1)}, u32[]{:S(2)}, u32[]{:S(2)}) %collective-permute-start) | collective-permute-done | bytes 262176 | tf_op jit(solution)/shard_map/while/body/eval_jaxpr/ppermute | solution.py:17
  523.2 8.5 %collective-permute-done = bf16[1,16,64,128]{3,2,1,0:T(8,128)(2,1)S(1)} collective-permute-done((bf16[1,16,64,128]{3,2,1,0:T(8,128)(2,1)S(1)}, bf16[1,16,64,128]{3,2,1,0:T(8,128)(2,1)S(1)}, u32[]{:S(2)}, u32[]{:S(2)}) %collective-permute-start) | collective-permute-done | bytes 262176 | tf_op jit(solution)/shard_map/while/body/eval_jaxpr/ppermute | solution.py:17
  545.6 8.5 %collective-permute-done = bf16[1,16,64,128]{3,2,1,0:T(8,128)(2,1)S(1)} collective-permute-done((bf16[1,16,64,128]{3,2,1,0:T(8,128)(2,1)S(1)}, bf16[1,16,64,128]{3,2,1,0:T(8,128)(2,1)S(1)}, u32[]{:S(2)}, u32[]{:S(2)}) %collective-permute-start) | collective-permute-done | bytes 262176 | tf_op jit(solution)/shard_map/while/body/eval_jaxpr/ppermute | solution.py:17
  556.9 8.5 %collective-permute-done = bf16[1,16,64,128]{3,2,1,0:T(8,128)(2,1)S(1)} collective-permute-done((bf16[1,16,64,128]{3,2,1,0:T(8,128)(2,1)S(1)}, bf16[1,16,64,128]{3,2,1,0:T(8,128)(2,1)S(1)}, u32[]{:S(2)}, u32[]{:S(2)}) %collective-permute-start) | collective-permute-done | bytes 262176 | tf_op jit(solution)/shard_map/while/body/eval_jaxpr/ppermute | solution.py:17
  579.3 8.5 %collective-permute-done = bf16[1,16,64,128]{3,2,1,0:T(8,128)(2,1)S(1)} collective-permute-done((bf16[1,16,64,128]{3,2,1,0:T(8,128)(2,1)S(1)}, bf16[1,16,64,128]{3,2,1,0:T(8,128)(2,1)S(1)}, u32[]{:S(2)}, u32[]{:S(2)}) %collective-permute-start) | collective-permute-done | bytes 262176 | tf_op jit(solution)/shard_map/while/body/eval_jaxpr/ppermute | solution.py:17
  590.5 8.5 %collective-permute-done = bf16[1,16,64,128]{3,2,1,0:T(8,128)(2,1)S(1)} collective-permute-done((bf16[1,16,64,128]{3,2,1,0:T(8,128)(2,1)S(1)}, bf16[1,16,64,128]{3,2,1,0:T(8,128)(2,1)S(1)}, u32[]{:S(2)}, u32[]{:S(2)}) %collective-permute-start) | collective-permute-done | bytes 262176 | tf_op jit(solution)/shard_map/while/body/eval_jaxpr/ppermute | solution.py:17
  613.0 8.5 %collective-permute-done = bf16[1,16,64,128]{3,2,1,0:T(8,128)(2,1)S(1)} collective-permute-done((bf16[1,16,64,128]{3,2,1,0:T(8,128)(2,1)S(1)}, bf16[1,16,64,128]{3,2,1,0:T(8,128)(2,1)S(1)}, u32[]{:S(2)}, u32[]{:S(2)}) %collective-permute-start) | collective-permute-done | bytes 262176 | tf_op jit(solution)/shard_map/while/body/eval_jaxpr/ppermute | solution.py:17
  624.2 8.5 %collective-permute-done = bf16[1,16,64,128]{3,2,1,0:T(8,128)(2,1)S(1)} collective-permute-done((bf16[1,16,64,128]{3,2,1,0:T(8,128)(2,1)S(1)}, bf16[1,16,64,128]{3,2,1,0:T(8,128)(2,1)S(1)}, u32[]{:S(2)}, u32[]{:S(2)}) %collective-permute-start) | collective-permute-done | bytes 262176 | tf_op jit(solution)/shard_map/while/body/eval_jaxpr/ppermute | solution.py:17
  646.6 8.5 %collective-permute-done = bf16[1,16,64,128]{3,2,1,0:T(8,128)(2,1)S(1)} collective-permute-done((bf16[1,16,64,128]{3,2,1,0:T(8,128)(2,1)S(1)}, bf16[1,16,64,128]{3,2,1,0:T(8,128)(2,1)S(1)}, u32[]{:S(2)}, u32[]{:S(2)}) %collective-permute-start) | collective-permute-done | bytes 262176 | tf_op jit(solution)/shard_map/while/body/eval_jaxpr/ppermute | solution.py:17
  657.8 8.5 %collective-permute-done = bf16[1,16,64,128]{3,2,1,0:T(8,128)(2,1)S(1)} collective-permute-done((bf16[1,16,64,128]{3,2,1,0:T(8,128)(2,1)S(1)}, bf16[1,16,64,128]{3,2,1,0:T(8,128)(2,1)S(1)}, u32[]{:S(2)}, u32[]{:S(2)}) %collective-permute-start) | collective-permute-done | bytes 262176 | tf_op jit(solution)/shard_map/while/body/eval_jaxpr/ppermute | solution.py:17
  680.3 8.5 %collective-permute-done = bf16[1,16,64,128]{3,2,1,0:T(8,128)(2,1)S(1)} collective-permute-done((bf16[1,16,64,128]{3,2,1,0:T(8,128)(2,1)S(1)}, bf16[1,16,64,128]{3,2,1,0:T(8,128)(2,1)S(1)}, u32[]{:S(2)}, u32[]{:S(2)}) %collective-permute-start) | collective-permute-done | bytes 262176 | tf_op jit(solution)/shard_map/while/body/eval_jaxpr/ppermute | solution.py:17
  691.5 8.5 %collective-permute-done = bf16[1,16,64,128]{3,2,1,0:T(8,128)(2,1)S(1)} collective-permute-done((bf16[1,16,64,128]{3,2,1,0:T(8,128)(2,1)S(1)}, bf16[1,16,64,128]{3,2,1,0:T(8,128)(2,1)S(1)}, u32[]{:S(2)}, u32[]{:S(2)}) %collective-permute-start) | collective-permute-done | bytes 262176 | tf_op jit(solution)/shard_map/while/body/eval_jaxpr/ppermute | solution.py:17
  705.6 33.4 %psum.7 = f32[256]{0:T(256)S(1)} all-reduce(f32[256]{0:T(256)S(1)} %multiply_reduce_fusion), channel_id=1, replica_groups=mesh['ctx'=32,'tp'=8] {'tp'}, use_global_device_ids=true, to_apply=%region_11.12 | all-reduce | flops 256 | bytes 2048 | tf_op jit(solution)/shard_map/psum | solution.py:142
  (473 shorter events, 524.9 us)
Async XLA Ops:
  353.0 10.4 %collective-permute-start = (bf16[1,16,64,128]{3,2,1,0:T(8,128)(2,1)S(1)}, bf16[1,16,64,128]{3,2,1,0:T(8,128)(2,1)S(1)}, u32[]{:S(2)}, u32[]{:S(2)}) collective-permute-start(bf16[1,16,64,128]{3,2,1,0:T(8,128)(2,1)S(1)} %get-tuple-element.471), channel_id=1, source_target_pairs={{0,8},{8,16},{16,24},{24,32},{32,40},{40,48},{48,56},{56,64},{64,7... | collective-permute-start | bytes 786440 | tf_op jit(solution)/shard_map/while/body/eval_jaxpr/ppermute | solution.py:17
  364.2 10.4 %collective-permute-start = (bf16[1,16,64,128]{3,2,1,0:T(8,128)(2,1)S(1)}, bf16[1,16,64,128]{3,2,1,0:T(8,128)(2,1)S(1)}, u32[]{:S(2)}, u32[]{:S(2)}) collective-permute-start(bf16[1,16,64,128]{3,2,1,0:T(8,128)(2,1)S(1)} %get-tuple-element.471), channel_id=1, source_target_pairs={{0,8},{8,16},{16,24},{24,32},{32,40},{40,48},{48,56},{56,64},{64,7... | collective-permute-start | bytes 786440 | tf_op jit(solution)/shard_map/while/body/eval_jaxpr/ppermute | solution.py:17
  375.4 10.4 %collective-permute-start = (bf16[1,16,64,128]{3,2,1,0:T(8,128)(2,1)S(1)}, bf16[1,16,64,128]{3,2,1,0:T(8,128)(2,1)S(1)}, u32[]{:S(2)}, u32[]{:S(2)}) collective-permute-start(bf16[1,16,64,128]{3,2,1,0:T(8,128)(2,1)S(1)} %get-tuple-element.471), channel_id=1, source_target_pairs={{0,8},{8,16},{16,24},{24,32},{32,40},{40,48},{48,56},{56,64},{64,7... | collective-permute-start | bytes 786440 | tf_op jit(solution)/shard_map/while/body/eval_jaxpr/ppermute | solution.py:17
  386.7 10.4 %collective-permute-start = (bf16[1,16,64,128]{3,2,1,0:T(8,128)(2,1)S(1)}, bf16[1,16,64,128]{3,2,1,0:T(8,128)(2,1)S(1)}, u32[]{:S(2)}, u32[]{:S(2)}) collective-permute-start(bf16[1,16,64,128]{3,2,1,0:T(8,128)(2,1)S(1)} %get-tuple-element.471), channel_id=1, source_target_pairs={{0,8},{8,16},{16,24},{24,32},{32,40},{40,48},{48,56},{56,64},{64,7... | collective-permute-start | bytes 786440 | tf_op jit(solution)/shard_map/while/body/eval_jaxpr/ppermute | solution.py:17
  397.9 10.4 %collective-permute-start = (bf16[1,16,64,128]{3,2,1,0:T(8,128)(2,1)S(1)}, bf16[1,16,64,128]{3,2,1,0:T(8,128)(2,1)S(1)}, u32[]{:S(2)}, u32[]{:S(2)}) collective-permute-start(bf16[1,16,64,128]{3,2,1,0:T(8,128)(2,1)S(1)} %get-tuple-element.471), channel_id=1, source_target_pairs={{0,8},{8,16},{16,24},{24,32},{32,40},{40,48},{48,56},{56,64},{64,7... | collective-permute-start | bytes 786440 | tf_op jit(solution)/shard_map/while/body/eval_jaxpr/ppermute | solution.py:17
  409.1 10.4 %collective-permute-start = (bf16[1,16,64,128]{3,2,1,0:T(8,128)(2,1)S(1)}, bf16[1,16,64,128]{3,2,1,0:T(8,128)(2,1)S(1)}, u32[]{:S(2)}, u32[]{:S(2)}) collective-permute-start(bf16[1,16,64,128]{3,2,1,0:T(8,128)(2,1)S(1)} %get-tuple-element.471), channel_id=1, source_target_pairs={{0,8},{8,16},{16,24},{24,32},{32,40},{40,48},{48,56},{56,64},{64,7... | collective-permute-start | bytes 786440 | tf_op jit(solution)/shard_map/while/body/eval_jaxpr/ppermute | solution.py:17
  420.3 10.4 %collective-permute-start = (bf16[1,16,64,128]{3,2,1,0:T(8,128)(2,1)S(1)}, bf16[1,16,64,128]{3,2,1,0:T(8,128)(2,1)S(1)}, u32[]{:S(2)}, u32[]{:S(2)}) collective-permute-start(bf16[1,16,64,128]{3,2,1,0:T(8,128)(2,1)S(1)} %get-tuple-element.471), channel_id=1, source_target_pairs={{0,8},{8,16},{16,24},{24,32},{32,40},{40,48},{48,56},{56,64},{64,7... | collective-permute-start | bytes 786440 | tf_op jit(solution)/shard_map/while/body/eval_jaxpr/ppermute | solution.py:17
  431.5 10.4 %collective-permute-start = (bf16[1,16,64,128]{3,2,1,0:T(8,128)(2,1)S(1)}, bf16[1,16,64,128]{3,2,1,0:T(8,128)(2,1)S(1)}, u32[]{:S(2)}, u32[]{:S(2)}) collective-permute-start(bf16[1,16,64,128]{3,2,1,0:T(8,128)(2,1)S(1)} %get-tuple-element.471), channel_id=1, source_target_pairs={{0,8},{8,16},{16,24},{24,32},{32,40},{40,48},{48,56},{56,64},{64,7... | collective-permute-start | bytes 786440 | tf_op jit(solution)/shard_map/while/body/eval_jaxpr/ppermute | solution.py:17
  442.8 10.4 %collective-permute-start = (bf16[1,16,64,128]{3,2,1,0:T(8,128)(2,1)S(1)}, bf16[1,16,64,128]{3,2,1,0:T(8,128)(2,1)S(1)}, u32[]{:S(2)}, u32[]{:S(2)}) collective-permute-start(bf16[1,16,64,128]{3,2,1,0:T(8,128)(2,1)S(1)} %get-tuple-element.471), channel_id=1, source_target_pairs={{0,8},{8,16},{16,24},{24,32},{32,40},{40,48},{48,56},{56,64},{64,7... | collective-permute-start | bytes 786440 | tf_op jit(solution)/shard_map/while/body/eval_jaxpr/ppermute | solution.py:17
  454.0 10.4 %collective-permute-start = (bf16[1,16,64,128]{3,2,1,0:T(8,128)(2,1)S(1)}, bf16[1,16,64,128]{3,2,1,0:T(8,128)(2,1)S(1)}, u32[]{:S(2)}, u32[]{:S(2)}) collective-permute-start(bf16[1,16,64,128]{3,2,1,0:T(8,128)(2,1)S(1)} %get-tuple-element.471), channel_id=1, source_target_pairs={{0,8},{8,16},{16,24},{24,32},{32,40},{40,48},{48,56},{56,64},{64,7... | collective-permute-start | bytes 786440 | tf_op jit(solution)/shard_map/while/body/eval_jaxpr/ppermute | solution.py:17
  465.2 10.4 %collective-permute-start = (bf16[1,16,64,128]{3,2,1,0:T(8,128)(2,1)S(1)}, bf16[1,16,64,128]{3,2,1,0:T(8,128)(2,1)S(1)}, u32[]{:S(2)}, u32[]{:S(2)}) collective-permute-start(bf16[1,16,64,128]{3,2,1,0:T(8,128)(2,1)S(1)} %get-tuple-element.471), channel_id=1, source_target_pairs={{0,8},{8,16},{16,24},{24,32},{32,40},{40,48},{48,56},{56,64},{64,7... | collective-permute-start | bytes 786440 | tf_op jit(solution)/shard_map/while/body/eval_jaxpr/ppermute | solution.py:17
  476.4 10.4 %collective-permute-start = (bf16[1,16,64,128]{3,2,1,0:T(8,128)(2,1)S(1)}, bf16[1,16,64,128]{3,2,1,0:T(8,128)(2,1)S(1)}, u32[]{:S(2)}, u32[]{:S(2)}) collective-permute-start(bf16[1,16,64,128]{3,2,1,0:T(8,128)(2,1)S(1)} %get-tuple-element.471), channel_id=1, source_target_pairs={{0,8},{8,16},{16,24},{24,32},{32,40},{40,48},{48,56},{56,64},{64,7... | collective-permute-start | bytes 786440 | tf_op jit(solution)/shard_map/while/body/eval_jaxpr/ppermute | solution.py:17
  487.6 10.4 %collective-permute-start = (bf16[1,16,64,128]{3,2,1,0:T(8,128)(2,1)S(1)}, bf16[1,16,64,128]{3,2,1,0:T(8,128)(2,1)S(1)}, u32[]{:S(2)}, u32[]{:S(2)}) collective-permute-start(bf16[1,16,64,128]{3,2,1,0:T(8,128)(2,1)S(1)} %get-tuple-element.471), channel_id=1, source_target_pairs={{0,8},{8,16},{16,24},{24,32},{32,40},{40,48},{48,56},{56,64},{64,7... | collective-permute-start | bytes 786440 | tf_op jit(solution)/shard_map/while/body/eval_jaxpr/ppermute | solution.py:17
  498.8 10.4 %collective-permute-start = (bf16[1,16,64,128]{3,2,1,0:T(8,128)(2,1)S(1)}, bf16[1,16,64,128]{3,2,1,0:T(8,128)(2,1)S(1)}, u32[]{:S(2)}, u32[]{:S(2)}) collective-permute-start(bf16[1,16,64,128]{3,2,1,0:T(8,128)(2,1)S(1)} %get-tuple-element.471), channel_id=1, source_target_pairs={{0,8},{8,16},{16,24},{24,32},{32,40},{40,48},{48,56},{56,64},{64,7... | collective-permute-start | bytes 786440 | tf_op jit(solution)/shard_map/while/body/eval_jaxpr/ppermute | solution.py:17
  510.1 10.4 %collective-permute-start = (bf16[1,16,64,128]{3,2,1,0:T(8,128)(2,1)S(1)}, bf16[1,16,64,128]{3,2,1,0:T(8,128)(2,1)S(1)}, u32[]{:S(2)}, u32[]{:S(2)}) collective-permute-start(bf16[1,16,64,128]{3,2,1,0:T(8,128)(2,1)S(1)} %get-tuple-element.471), channel_id=1, source_target_pairs={{0,8},{8,16},{16,24},{24,32},{32,40},{40,48},{48,56},{56,64},{64,7... | collective-permute-start | bytes 786440 | tf_op jit(solution)/shard_map/while/body/eval_jaxpr/ppermute | solution.py:17
  521.3 10.4 %collective-permute-start = (bf16[1,16,64,128]{3,2,1,0:T(8,128)(2,1)S(1)}, bf16[1,16,64,128]{3,2,1,0:T(8,128)(2,1)S(1)}, u32[]{:S(2)}, u32[]{:S(2)}) collective-permute-start(bf16[1,16,64,128]{3,2,1,0:T(8,128)(2,1)S(1)} %get-tuple-element.471), channel_id=1, source_target_pairs={{0,8},{8,16},{16,24},{24,32},{32,40},{40,48},{48,56},{56,64},{64,7... | collective-permute-start | bytes 786440 | tf_op jit(solution)/shard_map/while/body/eval_jaxpr/ppermute | solution.py:17
  532.5 10.4 %collective-permute-start = (bf16[1,16,64,128]{3,2,1,0:T(8,128)(2,1)S(1)}, bf16[1,16,64,128]{3,2,1,0:T(8,128)(2,1)S(1)}, u32[]{:S(2)}, u32[]{:S(2)}) collective-permute-start(bf16[1,16,64,128]{3,2,1,0:T(8,128)(2,1)S(1)} %get-tuple-element.471), channel_id=1, source_target_pairs={{0,8},{8,16},{16,24},{24,32},{32,40},{40,48},{48,56},{56,64},{64,7... | collective-permute-start | bytes 786440 | tf_op jit(solution)/shard_map/while/body/eval_jaxpr/ppermute | solution.py:17
  554.9 10.4 %collective-permute-start = (bf16[1,16,64,128]{3,2,1,0:T(8,128)(2,1)S(1)}, bf16[1,16,64,128]{3,2,1,0:T(8,128)(2,1)S(1)}, u32[]{:S(2)}, u32[]{:S(2)}) collective-permute-start(bf16[1,16,64,128]{3,2,1,0:T(8,128)(2,1)S(1)} %get-tuple-element.471), channel_id=1, source_target_pairs={{0,8},{8,16},{16,24},{24,32},{32,40},{40,48},{48,56},{56,64},{64,7... | collective-permute-start | bytes 786440 | tf_op jit(solution)/shard_map/while/body/eval_jaxpr/ppermute | solution.py:17
  588.6 10.4 %collective-permute-start = (bf16[1,16,64,128]{3,2,1,0:T(8,128)(2,1)S(1)}, bf16[1,16,64,128]{3,2,1,0:T(8,128)(2,1)S(1)}, u32[]{:S(2)}, u32[]{:S(2)}) collective-permute-start(bf16[1,16,64,128]{3,2,1,0:T(8,128)(2,1)S(1)} %get-tuple-element.471), channel_id=1, source_target_pairs={{0,8},{8,16},{16,24},{24,32},{32,40},{40,48},{48,56},{56,64},{64,7... | collective-permute-start | bytes 786440 | tf_op jit(solution)/shard_map/while/body/eval_jaxpr/ppermute | solution.py:17
  622.3 10.4 %collective-permute-start = (bf16[1,16,64,128]{3,2,1,0:T(8,128)(2,1)S(1)}, bf16[1,16,64,128]{3,2,1,0:T(8,128)(2,1)S(1)}, u32[]{:S(2)}, u32[]{:S(2)}) collective-permute-start(bf16[1,16,64,128]{3,2,1,0:T(8,128)(2,1)S(1)} %get-tuple-element.471), channel_id=1, source_target_pairs={{0,8},{8,16},{16,24},{24,32},{32,40},{40,48},{48,56},{56,64},{64,7... | collective-permute-start | bytes 786440 | tf_op jit(solution)/shard_map/while/body/eval_jaxpr/ppermute | solution.py:17
  655.9 10.4 %collective-permute-start = (bf16[1,16,64,128]{3,2,1,0:T(8,128)(2,1)S(1)}, bf16[1,16,64,128]{3,2,1,0:T(8,128)(2,1)S(1)}, u32[]{:S(2)}, u32[]{:S(2)}) collective-permute-start(bf16[1,16,64,128]{3,2,1,0:T(8,128)(2,1)S(1)} %get-tuple-element.471), channel_id=1, source_target_pairs={{0,8},{8,16},{16,24},{24,32},{32,40},{40,48},{48,56},{56,64},{64,7... | collective-permute-start | bytes 786440 | tf_op jit(solution)/shard_map/while/body/eval_jaxpr/ppermute | solution.py:17
  667.1 10.4 %collective-permute-start = (bf16[1,16,64,128]{3,2,1,0:T(8,128)(2,1)S(1)}, bf16[1,16,64,128]{3,2,1,0:T(8,128)(2,1)S(1)}, u32[]{:S(2)}, u32[]{:S(2)}) collective-permute-start(bf16[1,16,64,128]{3,2,1,0:T(8,128)(2,1)S(1)} %get-tuple-element.471), channel_id=1, source_target_pairs={{0,8},{8,16},{16,24},{24,32},{32,40},{40,48},{48,56},{56,64},{64,7... | collective-permute-start | bytes 786440 | tf_op jit(solution)/shard_map/while/body/eval_jaxpr/ppermute | solution.py:17
  678.4 10.4 %collective-permute-start = (bf16[1,16,64,128]{3,2,1,0:T(8,128)(2,1)S(1)}, bf16[1,16,64,128]{3,2,1,0:T(8,128)(2,1)S(1)}, u32[]{:S(2)}, u32[]{:S(2)}) collective-permute-start(bf16[1,16,64,128]{3,2,1,0:T(8,128)(2,1)S(1)} %get-tuple-element.471), channel_id=1, source_target_pairs={{0,8},{8,16},{16,24},{24,32},{32,40},{40,48},{48,56},{56,64},{64,7... | collective-permute-start | bytes 786440 | tf_op jit(solution)/shard_map/while/body/eval_jaxpr/ppermute | solution.py:17
  689.6 10.4 %collective-permute-start = (bf16[1,16,64,128]{3,2,1,0:T(8,128)(2,1)S(1)}, bf16[1,16,64,128]{3,2,1,0:T(8,128)(2,1)S(1)}, u32[]{:S(2)}, u32[]{:S(2)}) collective-permute-start(bf16[1,16,64,128]{3,2,1,0:T(8,128)(2,1)S(1)} %get-tuple-element.471), channel_id=1, source_target_pairs={{0,8},{8,16},{16,24},{24,32},{32,40},{40,48},{48,56},{56,64},{64,7... | collective-permute-start | bytes 786440 | tf_op jit(solution)/shard_map/while/body/eval_jaxpr/ppermute | solution.py:17
  (48 other events, 1066.6 us)
where the time goes:
time: 743 us; the launch traced here: 740 us
  waiting for transfers between devices  477 us (64%)
  starting transfers between devices  119 us (16%)
  matrix products  52.5 us (7%)
  other arithmetic  50.4 us (7%)
  blocking collectives  33.4 us (4%)
    ppermute x62, waiting for transfers between devices, passed_along(): return lax.ppermute(block, axis, route)  477 us
    ppermute x62, starting transfers between devices, passed_along(): return lax.ppermute(block, axis, route)  119 us
    psum x1, blocking collectives, local(): square_total = lax.psum(jnp.sum(gated * gated, axis=-1), 'tp')  33.4 us
    dot_general x32, matrix products, sub_step(): jnp.einsum('wlhc,cwm->wlhm', weights.astype(jnp.bfloat16), value_portion,...  33 us
    add x31, other arithmetic, relay_step(): return (received, block_decay[..., None, None] * received + local_state)  26.1 us
    reduce_sum x32, other arithmetic, sub_step(): run_sum = run_sum * correction_factor + jnp.sum(weights, axis=-1)  16.5 us
    dot_general x32, matrix products, sub_step(): jnp.einsum('faqo,bao->aqfb', query_head_rows, key_portion, preferred_elem...  15.9 us
  transfers between devices with their start and end apart: 62, of which 62 were waited for; matrix products, arithmetic and copies ran while one was open for 0% of the time, Pallas kernels for 0%

commit v1 on v0

--- a/solution.py
+++ b/solution.py
@@ -139,7 +139,13 @@
     )
     outputs = (inner + carried_out + direct).reshape(tok_rows, -1)
     gated = outputs * jax.nn.silu(gate_input.astype(jnp.float32))
-    square_total = lax.psum(jnp.sum(gated * gated, axis=-1), "tp")
+
+    def drive_rows(frame):
+        raw_out = lax.all_gather(frame, "tp")
+        b_now = jnp.sum(raw_out, axis=0)
+        return b_now
+
+    square_total = drive_rows(jnp.sum(gated * gated, axis=-1))
     scaling = lax.rsqrt(square_total / (STATE_HEADS * P_SIZE) + 1e-05)
     mixer_out = (gated * scaling[:, None] * norm_gain.astype(jnp.float32)).astype(jnp.bfloat16)
     return (attention_out, mixer_out)

time: 743 us -> 742 us (level)
    psum x1 -> x0, blocking collectives: 33.4 us -> none  [local(): square_total = lax.psum(jnp.sum(gated * gated, axis=-1), 'tp')]
    all_gather x0 -> x1, blocking collectives: none -> 32.6 us  [drive_rows(): raw_out = lax.all_gather(frame, 'tp')]
where the time goes in v1:
time: 742 us; the launch traced here: 739 us
  waiting for transfers between devices  477 us (64%)
  starting transfers between devices  119 us (16%)
  matrix products  52.5 us (7%)
  other arithmetic  50.5 us (7%)
  blocking collectives  32.6 us (4%)
    ppermute x62, waiting for transfers between devices, passed_along(): return lax.ppermute(block, axis, route)  477 us
    ppermute x62, starting transfers between devices, passed_along(): return lax.ppermute(block, axis, route)  119 us
    dot_general x32, matrix products, sub_step(): jnp.einsum('wlhc,cwm->wlhm', weights.astype(jnp.bfloat16), value_portion,...  33 us
    all_gather x1, blocking collectives, drive_rows(): raw_out = lax.all_gather(frame, 'tp')  32.6 us
    add x31, other arithmetic, relay_step(): return (received, block_decay[..., None, None] * received + local_state)  26.1 us
    reduce_sum x32, other arithmetic, sub_step(): run_sum = run_sum * correction_factor + jnp.sum(weights, axis=-1)  16.5 us
    dot_general x32, matrix products, sub_step(): jnp.einsum('faqo,bao->aqfb', query_head_rows, key_portion, preferred_elem...  15.9 us
  transfers between devices with their start and end apart: 62, of which 62 were waited for; matrix products, arithmetic and copies ran while one was open for 0% of the time, Pallas kernels for 0%

profile of v1, /device:TPU:2, one launch (start us, length us, event | category | flops | bytes accessed | tf_op | source)
XLA Modules:
  0.0 739.3 jit_solution(33844709612663921)
XLA Ops:
  5.4 343.8 %while.55 = (s32[]{:T(128)}, bf16[2,256,128]{2,1,0:T(8,128)(2,1)S(1)}, f32[1,8,256]{2,1,0:T(8,128)S(1)}, f32[1,8,256]{2,1,0:T(8,128)S(1)}, f32[1,8,256,128]{3,2,...) while((s32[]{:T(128)}, ...), condition=%wide.region_5.6_spmd.clone, body=%wide.region_2.5_spmd.clone.sunk | while | flops 275847680 | bytes 10227923 | solution.py:94
  353.0 347.9 %while.54 = (s32[]{:T(128)}, f32[1,16,64,128]{3,2,1,0:T(8,128)}, bf16[1,16,64,128]{3,2,1,0:T(8,128)(2,1)S(1)}, f32[1,16]{1,0:T(1,128)S(1)}, f32[1,16,64,128]{3,2,1,0:T(8,128)S(1)}, /*index=5*/s32[]{:T(128)}) while((s32[]{:T(128)}, f32[1,16,64,128]{3,2,1,0:T(8,128)}, bf16[1,16,64,128]{3,2,1,0:T(8,128)(2,1)S(1)}, f32[1,16]{1,0:T(1,128)S(1)}, ...), condition=%wide.region_9.10_spmd, body=%wide.region_8.9_spmd.sunk | while | flops 524290 | bytes 2621613 | solution.py:130
  366.1 8.5 %collective-permute-done = bf16[1,16,64,128]{3,2,1,0:T(8,128)(2,1)S(1)} collective-permute-done((bf16[1,16,64,128]{3,2,1,0:T(8,128)(2,1)S(1)}, bf16[1,16,64,128]{3,2,1,0:T(8,128)(2,1)S(1)}, u32[]{:S(2)}, u32[]{:S(2)}) %collective-permute-start) | collective-permute-done | bytes 262176 | tf_op jit(solution)/shard_map/while/body/eval_jaxpr/ppermute | solution.py:17
  377.4 8.5 %collective-permute-done = bf16[1,16,64,128]{3,2,1,0:T(8,128)(2,1)S(1)} collective-permute-done((bf16[1,16,64,128]{3,2,1,0:T(8,128)(2,1)S(1)}, bf16[1,16,64,128]{3,2,1,0:T(8,128)(2,1)S(1)}, u32[]{:S(2)}, u32[]{:S(2)}) %collective-permute-start) | collective-permute-done | bytes 262176 | tf_op jit(solution)/shard_map/while/body/eval_jaxpr/ppermute | solution.py:17
  399.8 8.5 %collective-permute-done = bf16[1,16,64,128]{3,2,1,0:T(8,128)(2,1)S(1)} collective-permute-done((bf16[1,16,64,128]{3,2,1,0:T(8,128)(2,1)S(1)}, bf16[1,16,64,128]{3,2,1,0:T(8,128)(2,1)S(1)}, u32[]{:S(2)}, u32[]{:S(2)}) %collective-permute-start) | collective-permute-done | bytes 262176 | tf_op jit(solution)/shard_map/while/body/eval_jaxpr/ppermute | solution.py:17
  411.0 8.5 %collective-permute-done = bf16[1,16,64,128]{3,2,1,0:T(8,128)(2,1)S(1)} collective-permute-done((bf16[1,16,64,128]{3,2,1,0:T(8,128)(2,1)S(1)}, bf16[1,16,64,128]{3,2,1,0:T(8,128)(2,1)S(1)}, u32[]{:S(2)}, u32[]{:S(2)}) %collective-permute-start) | collective-permute-done | bytes 262176 | tf_op jit(solution)/shard_map/while/body/eval_jaxpr/ppermute | solution.py:17
  433.4 8.5 %collective-permute-done = bf16[1,16,64,128]{3,2,1,0:T(8,128)(2,1)S(1)} collective-permute-done((bf16[1,16,64,128]{3,2,1,0:T(8,128)(2,1)S(1)}, bf16[1,16,64,128]{3,2,1,0:T(8,128)(2,1)S(1)}, u32[]{:S(2)}, u32[]{:S(2)}) %collective-permute-start) | collective-permute-done | bytes 262176 | tf_op jit(solution)/shard_map/while/body/eval_jaxpr/ppermute | solution.py:17
  444.7 8.5 %collective-permute-done = bf16[1,16,64,128]{3,2,1,0:T(8,128)(2,1)S(1)} collective-permute-done((bf16[1,16,64,128]{3,2,1,0:T(8,128)(2,1)S(1)}, bf16[1,16,64,128]{3,2,1,0:T(8,128)(2,1)S(1)}, u32[]{:S(2)}, u32[]{:S(2)}) %collective-permute-start) | collective-permute-done | bytes 262176 | tf_op jit(solution)/shard_map/while/body/eval_jaxpr/ppermute | solution.py:17
  455.9 8.5 %collective-permute-done = bf16[1,16,64,128]{3,2,1,0:T(8,128)(2,1)S(1)} collective-permute-done((bf16[1,16,64,128]{3,2,1,0:T(8,128)(2,1)S(1)}, bf16[1,16,64,128]{3,2,1,0:T(8,128)(2,1)S(1)}, u32[]{:S(2)}, u32[]{:S(2)}) %collective-permute-start) | collective-permute-done | bytes 262176 | tf_op jit(solution)/shard_map/while/body/eval_jaxpr/ppermute | solution.py:17
  478.3 8.5 %collective-permute-done = bf16[1,16,64,128]{3,2,1,0:T(8,128)(2,1)S(1)} collective-permute-done((bf16[1,16,64,128]{3,2,1,0:T(8,128)(2,1)S(1)}, bf16[1,16,64,128]{3,2,1,0:T(8,128)(2,1)S(1)}, u32[]{:S(2)}, u32[]{:S(2)}) %collective-permute-start) | collective-permute-done | bytes 262176 | tf_op jit(solution)/shard_map/while/body/eval_jaxpr/ppermute | solution.py:17
  489.5 8.5 %collective-permute-done = bf16[1,16,64,128]{3,2,1,0:T(8,128)(2,1)S(1)} collective-permute-done((bf16[1,16,64,128]{3,2,1,0:T(8,128)(2,1)S(1)}, bf16[1,16,64,128]{3,2,1,0:T(8,128)(2,1)S(1)}, u32[]{:S(2)}, u32[]{:S(2)}) %collective-permute-start) | collective-permute-done | bytes 262176 | tf_op jit(solution)/shard_map/while/body/eval_jaxpr/ppermute | solution.py:17
  512.0 8.5 %collective-permute-done = bf16[1,16,64,128]{3,2,1,0:T(8,128)(2,1)S(1)} collective-permute-done((bf16[1,16,64,128]{3,2,1,0:T(8,128)(2,1)S(1)}, bf16[1,16,64,128]{3,2,1,0:T(8,128)(2,1)S(1)}, u32[]{:S(2)}, u32[]{:S(2)}) %collective-permute-start) | collective-permute-done | bytes 262176 | tf_op jit(solution)/shard_map/while/body/eval_jaxpr/ppermute | solution.py:17
  523.2 8.5 %collective-permute-done = bf16[1,16,64,128]{3,2,1,0:T(8,128)(2,1)S(1)} collective-permute-done((bf16[1,16,64,128]{3,2,1,0:T(8,128)(2,1)S(1)}, bf16[1,16,64,128]{3,2,1,0:T(8,128)(2,1)S(1)}, u32[]{:S(2)}, u32[]{:S(2)}) %collective-permute-start) | collective-permute-done | bytes 262176 | tf_op jit(solution)/shard_map/while/body/eval_jaxpr/ppermute | solution.py:17
  545.6 8.5 %collective-permute-done = bf16[1,16,64,128]{3,2,1,0:T(8,128)(2,1)S(1)} collective-permute-done((bf16[1,16,64,128]{3,2,1,0:T(8,128)(2,1)S(1)}, bf16[1,16,64,128]{3,2,1,0:T(8,128)(2,1)S(1)}, u32[]{:S(2)}, u32[]{:S(2)}) %collective-permute-start) | collective-permute-done | bytes 262176 | tf_op jit(solution)/shard_map/while/body/eval_jaxpr/ppermute | solution.py:17
  556.9 8.5 %collective-permute-done = bf16[1,16,64,128]{3,2,1,0:T(8,128)(2,1)S(1)} collective-permute-done((bf16[1,16,64,128]{3,2,1,0:T(8,128)(2,1)S(1)}, bf16[1,16,64,128]{3,2,1,0:T(8,128)(2,1)S(1)}, u32[]{:S(2)}, u32[]{:S(2)}) %collective-permute-start) | collective-permute-done | bytes 262176 | tf_op jit(solution)/shard_map/while/body/eval_jaxpr/ppermute | solution.py:17
  579.3 8.5 %collective-permute-done = bf16[1,16,64,128]{3,2,1,0:T(8,128)(2,1)S(1)} collective-permute-done((bf16[1,16,64,128]{3,2,1,0:T(8,128)(2,1)S(1)}, bf16[1,16,64,128]{3,2,1,0:T(8,128)(2,1)S(1)}, u32[]{:S(2)}, u32[]{:S(2)}) %collective-permute-start) | collective-permute-done | bytes 262176 | tf_op jit(solution)/shard_map/while/body/eval_jaxpr/ppermute | solution.py:17
  590.5 8.5 %collective-permute-done = bf16[1,16,64,128]{3,2,1,0:T(8,128)(2,1)S(1)} collective-permute-done((bf16[1,16,64,128]{3,2,1,0:T(8,128)(2,1)S(1)}, bf16[1,16,64,128]{3,2,1,0:T(8,128)(2,1)S(1)}, u32[]{:S(2)}, u32[]{:S(2)}) %collective-permute-start) | collective-permute-done | bytes 262176 | tf_op jit(solution)/shard_map/while/body/eval_jaxpr/ppermute | solution.py:17
  613.0 8.5 %collective-permute-done = bf16[1,16,64,128]{3,2,1,0:T(8,128)(2,1)S(1)} collective-permute-done((bf16[1,16,64,128]{3,2,1,0:T(8,128)(2,1)S(1)}, bf16[1,16,64,128]{3,2,1,0:T(8,128)(2,1)S(1)}, u32[]{:S(2)}, u32[]{:S(2)}) %collective-permute-start) | collective-permute-done | bytes 262176 | tf_op jit(solution)/shard_map/while/body/eval_jaxpr/ppermute | solution.py:17
  624.2 8.5 %collective-permute-done = bf16[1,16,64,128]{3,2,1,0:T(8,128)(2,1)S(1)} collective-permute-done((bf16[1,16,64,128]{3,2,1,0:T(8,128)(2,1)S(1)}, bf16[1,16,64,128]{3,2,1,0:T(8,128)(2,1)S(1)}, u32[]{:S(2)}, u32[]{:S(2)}) %collective-permute-start) | collective-permute-done | bytes 262176 | tf_op jit(solution)/shard_map/while/body/eval_jaxpr/ppermute | solution.py:17
  646.6 8.5 %collective-permute-done = bf16[1,16,64,128]{3,2,1,0:T(8,128)(2,1)S(1)} collective-permute-done((bf16[1,16,64,128]{3,2,1,0:T(8,128)(2,1)S(1)}, bf16[1,16,64,128]{3,2,1,0:T(8,128)(2,1)S(1)}, u32[]{:S(2)}, u32[]{:S(2)}) %collective-permute-start) | collective-permute-done | bytes 262176 | tf_op jit(solution)/shard_map/while/body/eval_jaxpr/ppermute | solution.py:17
  657.8 8.5 %collective-permute-done = bf16[1,16,64,128]{3,2,1,0:T(8,128)(2,1)S(1)} collective-permute-done((bf16[1,16,64,128]{3,2,1,0:T(8,128)(2,1)S(1)}, bf16[1,16,64,128]{3,2,1,0:T(8,128)(2,1)S(1)}, u32[]{:S(2)}, u32[]{:S(2)}) %collective-permute-start) | collective-permute-done | bytes 262176 | tf_op jit(solution)/shard_map/while/body/eval_jaxpr/ppermute | solution.py:17
  680.3 8.5 %collective-permute-done = bf16[1,16,64,128]{3,2,1,0:T(8,128)(2,1)S(1)} collective-permute-done((bf16[1,16,64,128]{3,2,1,0:T(8,128)(2,1)S(1)}, bf16[1,16,64,128]{3,2,1,0:T(8,128)(2,1)S(1)}, u32[]{:S(2)}, u32[]{:S(2)}) %collective-permute-start) | collective-permute-done | bytes 262176 | tf_op jit(solution)/shard_map/while/body/eval_jaxpr/ppermute | solution.py:17
  691.5 8.5 %collective-permute-done = bf16[1,16,64,128]{3,2,1,0:T(8,128)(2,1)S(1)} collective-permute-done((bf16[1,16,64,128]{3,2,1,0:T(8,128)(2,1)S(1)}, bf16[1,16,64,128]{3,2,1,0:T(8,128)(2,1)S(1)}, u32[]{:S(2)}, u32[]{:S(2)}) %collective-permute-start) | collective-permute-done | bytes 262176 | tf_op jit(solution)/shard_map/while/body/eval_jaxpr/ppermute | solution.py:17
  705.6 32.6 %all-gather.1 = f32[8,1,256]{2,1,0:T(1,128)S(1)} all-gather(f32[1,1,256]{2,1,0:T(1,128)S(1)} %bitcast.215), channel_id=2, replica_groups=mesh['ctx'=32,'tp'=8] {'tp'}, dimensions={0}, use_global_device_ids=true | all-gather | bytes 9216 | tf_op jit(solution)/shard_map/all_gather | solution.py:144
  (474 shorter events, 524.9 us)
Async XLA Ops:
  353.0 10.4 %collective-permute-start = (bf16[1,16,64,128]{3,2,1,0:T(8,128)(2,1)S(1)}, bf16[1,16,64,128]{3,2,1,0:T(8,128)(2,1)S(1)}, u32[]{:S(2)}, u32[]{:S(2)}) collective-permute-start(bf16[1,16,64,128]{3,2,1,0:T(8,128)(2,1)S(1)} %get-tuple-element.479), channel_id=1, source_target_pairs={{0,8},{8,16},{16,24},{24,32},{32,40},{40,48},{48,56},{56,64},{64,7... | collective-permute-start | bytes 786440 | tf_op jit(solution)/shard_map/while/body/eval_jaxpr/ppermute | solution.py:17
  364.2 10.4 %collective-permute-start = (bf16[1,16,64,128]{3,2,1,0:T(8,128)(2,1)S(1)}, bf16[1,16,64,128]{3,2,1,0:T(8,128)(2,1)S(1)}, u32[]{:S(2)}, u32[]{:S(2)}) collective-permute-start(bf16[1,16,64,128]{3,2,1,0:T(8,128)(2,1)S(1)} %get-tuple-element.479), channel_id=1, source_target_pairs={{0,8},{8,16},{16,24},{24,32},{32,40},{40,48},{48,56},{56,64},{64,7... | collective-permute-start | bytes 786440 | tf_op jit(solution)/shard_map/while/body/eval_jaxpr/ppermute | solution.py:17
  375.4 10.4 %collective-permute-start = (bf16[1,16,64,128]{3,2,1,0:T(8,128)(2,1)S(1)}, bf16[1,16,64,128]{3,2,1,0:T(8,128)(2,1)S(1)}, u32[]{:S(2)}, u32[]{:S(2)}) collective-permute-start(bf16[1,16,64,128]{3,2,1,0:T(8,128)(2,1)S(1)} %get-tuple-element.479), channel_id=1, source_target_pairs={{0,8},{8,16},{16,24},{24,32},{32,40},{40,48},{48,56},{56,64},{64,7... | collective-permute-start | bytes 786440 | tf_op jit(solution)/shard_map/while/body/eval_jaxpr/ppermute | solution.py:17
  386.7 10.4 %collective-permute-start = (bf16[1,16,64,128]{3,2,1,0:T(8,128)(2,1)S(1)}, bf16[1,16,64,128]{3,2,1,0:T(8,128)(2,1)S(1)}, u32[]{:S(2)}, u32[]{:S(2)}) collective-permute-start(bf16[1,16,64,128]{3,2,1,0:T(8,128)(2,1)S(1)} %get-tuple-element.479), channel_id=1, source_target_pairs={{0,8},{8,16},{16,24},{24,32},{32,40},{40,48},{48,56},{56,64},{64,7... | collective-permute-start | bytes 786440 | tf_op jit(solution)/shard_map/while/body/eval_jaxpr/ppermute | solution.py:17
  397.9 10.4 %collective-permute-start = (bf16[1,16,64,128]{3,2,1,0:T(8,128)(2,1)S(1)}, bf16[1,16,64,128]{3,2,1,0:T(8,128)(2,1)S(1)}, u32[]{:S(2)}, u32[]{:S(2)}) collective-permute-start(bf16[1,16,64,128]{3,2,1,0:T(8,128)(2,1)S(1)} %get-tuple-element.479), channel_id=1, source_target_pairs={{0,8},{8,16},{16,24},{24,32},{32,40},{40,48},{48,56},{56,64},{64,7... | collective-permute-start | bytes 786440 | tf_op jit(solution)/shard_map/while/body/eval_jaxpr/ppermute | solution.py:17
  409.1 10.4 %collective-permute-start = (bf16[1,16,64,128]{3,2,1,0:T(8,128)(2,1)S(1)}, bf16[1,16,64,128]{3,2,1,0:T(8,128)(2,1)S(1)}, u32[]{:S(2)}, u32[]{:S(2)}) collective-permute-start(bf16[1,16,64,128]{3,2,1,0:T(8,128)(2,1)S(1)} %get-tuple-element.479), channel_id=1, source_target_pairs={{0,8},{8,16},{16,24},{24,32},{32,40},{40,48},{48,56},{56,64},{64,7... | collective-permute-start | bytes 786440 | tf_op jit(solution)/shard_map/while/body/eval_jaxpr/ppermute | solution.py:17
  420.3 10.4 %collective-permute-start = (bf16[1,16,64,128]{3,2,1,0:T(8,128)(2,1)S(1)}, bf16[1,16,64,128]{3,2,1,0:T(8,128)(2,1)S(1)}, u32[]{:S(2)}, u32[]{:S(2)}) collective-permute-start(bf16[1,16,64,128]{3,2,1,0:T(8,128)(2,1)S(1)} %get-tuple-element.479), channel_id=1, source_target_pairs={{0,8},{8,16},{16,24},{24,32},{32,40},{40,48},{48,56},{56,64},{64,7... | collective-permute-start | bytes 786440 | tf_op jit(solution)/shard_map/while/body/eval_jaxpr/ppermute | solution.py:17
  431.5 10.4 %collective-permute-start = (bf16[1,16,64,128]{3,2,1,0:T(8,128)(2,1)S(1)}, bf16[1,16,64,128]{3,2,1,0:T(8,128)(2,1)S(1)}, u32[]{:S(2)}, u32[]{:S(2)}) collective-permute-start(bf16[1,16,64,128]{3,2,1,0:T(8,128)(2,1)S(1)} %get-tuple-element.479), channel_id=1, source_target_pairs={{0,8},{8,16},{16,24},{24,32},{32,40},{40,48},{48,56},{56,64},{64,7... | collective-permute-start | bytes 786440 | tf_op jit(solution)/shard_map/while/body/eval_jaxpr/ppermute | solution.py:17
  442.8 10.4 %collective-permute-start = (bf16[1,16,64,128]{3,2,1,0:T(8,128)(2,1)S(1)}, bf16[1,16,64,128]{3,2,1,0:T(8,128)(2,1)S(1)}, u32[]{:S(2)}, u32[]{:S(2)}) collective-permute-start(bf16[1,16,64,128]{3,2,1,0:T(8,128)(2,1)S(1)} %get-tuple-element.479), channel_id=1, source_target_pairs={{0,8},{8,16},{16,24},{24,32},{32,40},{40,48},{48,56},{56,64},{64,7... | collective-permute-start | bytes 786440 | tf_op jit(solution)/shard_map/while/body/eval_jaxpr/ppermute | solution.py:17
  454.0 10.4 %collective-permute-start = (bf16[1,16,64,128]{3,2,1,0:T(8,128)(2,1)S(1)}, bf16[1,16,64,128]{3,2,1,0:T(8,128)(2,1)S(1)}, u32[]{:S(2)}, u32[]{:S(2)}) collective-permute-start(bf16[1,16,64,128]{3,2,1,0:T(8,128)(2,1)S(1)} %get-tuple-element.479), channel_id=1, source_target_pairs={{0,8},{8,16},{16,24},{24,32},{32,40},{40,48},{48,56},{56,64},{64,7... | collective-permute-start | bytes 786440 | tf_op jit(solution)/shard_map/while/body/eval_jaxpr/ppermute | solution.py:17
  465.2 10.4 %collective-permute-start = (bf16[1,16,64,128]{3,2,1,0:T(8,128)(2,1)S(1)}, bf16[1,16,64,128]{3,2,1,0:T(8,128)(2,1)S(1)}, u32[]{:S(2)}, u32[]{:S(2)}) collective-permute-start(bf16[1,16,64,128]{3,2,1,0:T(8,128)(2,1)S(1)} %get-tuple-element.479), channel_id=1, source_target_pairs={{0,8},{8,16},{16,24},{24,32},{32,40},{40,48},{48,56},{56,64},{64,7... | collective-permute-start | bytes 786440 | tf_op jit(solution)/shard_map/while/body/eval_jaxpr/ppermute | solution.py:17
  476.4 10.4 %collective-permute-start = (bf16[1,16,64,128]{3,2,1,0:T(8,128)(2,1)S(1)}, bf16[1,16,64,128]{3,2,1,0:T(8,128)(2,1)S(1)}, u32[]{:S(2)}, u32[]{:S(2)}) collective-permute-start(bf16[1,16,64,128]{3,2,1,0:T(8,128)(2,1)S(1)} %get-tuple-element.479), channel_id=1, source_target_pairs={{0,8},{8,16},{16,24},{24,32},{32,40},{40,48},{48,56},{56,64},{64,7... | collective-permute-start | bytes 786440 | tf_op jit(solution)/shard_map/while/body/eval_jaxpr/ppermute | solution.py:17
  487.6 10.4 %collective-permute-start = (bf16[1,16,64,128]{3,2,1,0:T(8,128)(2,1)S(1)}, bf16[1,16,64,128]{3,2,1,0:T(8,128)(2,1)S(1)}, u32[]{:S(2)}, u32[]{:S(2)}) collective-permute-start(bf16[1,16,64,128]{3,2,1,0:T(8,128)(2,1)S(1)} %get-tuple-element.479), channel_id=1, source_target_pairs={{0,8},{8,16},{16,24},{24,32},{32,40},{40,48},{48,56},{56,64},{64,7... | collective-permute-start | bytes 786440 | tf_op jit(solution)/shard_map/while/body/eval_jaxpr/ppermute | solution.py:17
  498.8 10.4 %collective-permute-start = (bf16[1,16,64,128]{3,2,1,0:T(8,128)(2,1)S(1)}, bf16[1,16,64,128]{3,2,1,0:T(8,128)(2,1)S(1)}, u32[]{:S(2)}, u32[]{:S(2)}) collective-permute-start(bf16[1,16,64,128]{3,2,1,0:T(8,128)(2,1)S(1)} %get-tuple-element.479), channel_id=1, source_target_pairs={{0,8},{8,16},{16,24},{24,32},{32,40},{40,48},{48,56},{56,64},{64,7... | collective-permute-start | bytes 786440 | tf_op jit(solution)/shard_map/while/body/eval_jaxpr/ppermute | solution.py:17
  510.1 10.4 %collective-permute-start = (bf16[1,16,64,128]{3,2,1,0:T(8,128)(2,1)S(1)}, bf16[1,16,64,128]{3,2,1,0:T(8,128)(2,1)S(1)}, u32[]{:S(2)}, u32[]{:S(2)}) collective-permute-start(bf16[1,16,64,128]{3,2,1,0:T(8,128)(2,1)S(1)} %get-tuple-element.479), channel_id=1, source_target_pairs={{0,8},{8,16},{16,24},{24,32},{32,40},{40,48},{48,56},{56,64},{64,7... | collective-permute-start | bytes 786440 | tf_op jit(solution)/shard_map/while/body/eval_jaxpr/ppermute | solution.py:17
  521.3 10.4 %collective-permute-start = (bf16[1,16,64,128]{3,2,1,0:T(8,128)(2,1)S(1)}, bf16[1,16,64,128]{3,2,1,0:T(8,128)(2,1)S(1)}, u32[]{:S(2)}, u32[]{:S(2)}) collective-permute-start(bf16[1,16,64,128]{3,2,1,0:T(8,128)(2,1)S(1)} %get-tuple-element.479), channel_id=1, source_target_pairs={{0,8},{8,16},{16,24},{24,32},{32,40},{40,48},{48,56},{56,64},{64,7... | collective-permute-start | bytes 786440 | tf_op jit(solution)/shard_map/while/body/eval_jaxpr/ppermute | solution.py:17
  532.5 10.4 %collective-permute-start = (bf16[1,16,64,128]{3,2,1,0:T(8,128)(2,1)S(1)}, bf16[1,16,64,128]{3,2,1,0:T(8,128)(2,1)S(1)}, u32[]{:S(2)}, u32[]{:S(2)}) collective-permute-start(bf16[1,16,64,128]{3,2,1,0:T(8,128)(2,1)S(1)} %get-tuple-element.479), channel_id=1, source_target_pairs={{0,8},{8,16},{16,24},{24,32},{32,40},{40,48},{48,56},{56,64},{64,7... | collective-permute-start | bytes 786440 | tf_op jit(solution)/shard_map/while/body/eval_jaxpr/ppermute | solution.py:17
  554.9 10.4 %collective-permute-start = (bf16[1,16,64,128]{3,2,1,0:T(8,128)(2,1)S(1)}, bf16[1,16,64,128]{3,2,1,0:T(8,128)(2,1)S(1)}, u32[]{:S(2)}, u32[]{:S(2)}) collective-permute-start(bf16[1,16,64,128]{3,2,1,0:T(8,128)(2,1)S(1)} %get-tuple-element.479), channel_id=1, source_target_pairs={{0,8},{8,16},{16,24},{24,32},{32,40},{40,48},{48,56},{56,64},{64,7... | collective-permute-start | bytes 786440 | tf_op jit(solution)/shard_map/while/body/eval_jaxpr/ppermute | solution.py:17
  588.6 10.4 %collective-permute-start = (bf16[1,16,64,128]{3,2,1,0:T(8,128)(2,1)S(1)}, bf16[1,16,64,128]{3,2,1,0:T(8,128)(2,1)S(1)}, u32[]{:S(2)}, u32[]{:S(2)}) collective-permute-start(bf16[1,16,64,128]{3,2,1,0:T(8,128)(2,1)S(1)} %get-tuple-element.479), channel_id=1, source_target_pairs={{0,8},{8,16},{16,24},{24,32},{32,40},{40,48},{48,56},{56,64},{64,7... | collective-permute-start | bytes 786440 | tf_op jit(solution)/shard_map/while/body/eval_jaxpr/ppermute | solution.py:17
  622.3 10.4 %collective-permute-start = (bf16[1,16,64,128]{3,2,1,0:T(8,128)(2,1)S(1)}, bf16[1,16,64,128]{3,2,1,0:T(8,128)(2,1)S(1)}, u32[]{:S(2)}, u32[]{:S(2)}) collective-permute-start(bf16[1,16,64,128]{3,2,1,0:T(8,128)(2,1)S(1)} %get-tuple-element.479), channel_id=1, source_target_pairs={{0,8},{8,16},{16,24},{24,32},{32,40},{40,48},{48,56},{56,64},{64,7... | collective-permute-start | bytes 786440 | tf_op jit(solution)/shard_map/while/body/eval_jaxpr/ppermute | solution.py:17
  655.9 10.4 %collective-permute-start = (bf16[1,16,64,128]{3,2,1,0:T(8,128)(2,1)S(1)}, bf16[1,16,64,128]{3,2,1,0:T(8,128)(2,1)S(1)}, u32[]{:S(2)}, u32[]{:S(2)}) collective-permute-start(bf16[1,16,64,128]{3,2,1,0:T(8,128)(2,1)S(1)} %get-tuple-element.479), channel_id=1, source_target_pairs={{0,8},{8,16},{16,24},{24,32},{32,40},{40,48},{48,56},{56,64},{64,7... | collective-permute-start | bytes 786440 | tf_op jit(solution)/shard_map/while/body/eval_jaxpr/ppermute | solution.py:17
  667.1 10.4 %collective-permute-start = (bf16[1,16,64,128]{3,2,1,0:T(8,128)(2,1)S(1)}, bf16[1,16,64,128]{3,2,1,0:T(8,128)(2,1)S(1)}, u32[]{:S(2)}, u32[]{:S(2)}) collective-permute-start(bf16[1,16,64,128]{3,2,1,0:T(8,128)(2,1)S(1)} %get-tuple-element.479), channel_id=1, source_target_pairs={{0,8},{8,16},{16,24},{24,32},{32,40},{40,48},{48,56},{56,64},{64,7... | collective-permute-start | bytes 786440 | tf_op jit(solution)/shard_map/while/body/eval_jaxpr/ppermute | solution.py:17
  678.4 10.4 %collective-permute-start = (bf16[1,16,64,128]{3,2,1,0:T(8,128)(2,1)S(1)}, bf16[1,16,64,128]{3,2,1,0:T(8,128)(2,1)S(1)}, u32[]{:S(2)}, u32[]{:S(2)}) collective-permute-start(bf16[1,16,64,128]{3,2,1,0:T(8,128)(2,1)S(1)} %get-tuple-element.479), channel_id=1, source_target_pairs={{0,8},{8,16},{16,24},{24,32},{32,40},{40,48},{48,56},{56,64},{64,7... | collective-permute-start | bytes 786440 | tf_op jit(solution)/shard_map/while/body/eval_jaxpr/ppermute | solution.py:17
  689.6 10.4 %collective-permute-start = (bf16[1,16,64,128]{3,2,1,0:T(8,128)(2,1)S(1)}, bf16[1,16,64,128]{3,2,1,0:T(8,128)(2,1)S(1)}, u32[]{:S(2)}, u32[]{:S(2)}) collective-permute-start(bf16[1,16,64,128]{3,2,1,0:T(8,128)(2,1)S(1)} %get-tuple-element.479), channel_id=1, source_target_pairs={{0,8},{8,16},{16,24},{24,32},{32,40},{40,48},{48,56},{56,64},{64,7... | collective-permute-start | bytes 786440 | tf_op jit(solution)/shard_map/while/body/eval_jaxpr/ppermute | solution.py:17
  (48 other events, 1066.5 us)
